TPU v7x, 256 devices: a whole 4x4x8 slice. The times are simulated.
256 devices in a mesh: dp: 8 (over z_lo, x), expert: 32 (over z_hi, y, core).
Axes of the slice: x: 4, y: 4, z: 8 (z_hi: 4, z_lo: 2; z = z_hi * 2 + z_lo), core: 2. Of those that a mesh axis runs over, the one named last changes fastest.
Arguments:
- tokens: bfloat16 [8192, 4096], P('expert', 'dp'), may hold values from -6 to 6
- out_grad: bfloat16 [8192, 4096], P('expert', 'dp'), may hold values from -3 to 3
- expert_ids: int32 [8192, 2], P('expert'), may hold values from 0 to 31, as said below
- gate_probs: float32 [8192, 2], P('expert'), may hold values from 0.25 to 1
- w_gate: bfloat16 [32, 4096, 1024], P('expert', 'dp'), may hold values from -0.09375 to 0.09375
- w_up: bfloat16 [32, 4096, 1024], P('expert', 'dp'), may hold values from -0.09375 to 0.09375
- w_down: bfloat16 [32, 1024, 4096], P('expert', None, 'dp'), may hold values from -0.1875 to 0.1875
Outputs:
- token_grad: bfloat16 [8192, 4096], P('expert', 'dp')
- grad_w_gate: float32 [32, 4096, 1024], P('expert', 'dp')
- grad_w_up: float32 [32, 4096, 1024], P('expert', 'dp')
- grad_w_down: float32 [32, 1024, 4096], P('expert', None, 'dp')
Inputs may be any that keep to these rules, and one draw needn't show every extreme that they name: `expert_ids`: A token's two ids differ. Among the tokens of one aligned block of 256 tokens no expert is named more than 32 times; 4 experts, the same for every block, are named exactly 32 times in each block.
All inputs are finite; a program needn't handle non-finite values.
Results may differ from a plain program's by a relative error of at most 0.02.
Values may be sent and summed in bfloat16 or wider, within the bound.
No kernel may reach another device: no remote copies, remote signals or barrier semaphores. Data moves between devices by JAX's collectives and lax.ppermute only.
A program may use at most 64 MiB of HBM per device.

v0:
```python
import jax
import jax.numpy as jnp
from jax import lax
from jax.sharding import PartitionSpec as P

MOST = 32
contract_rows = (((0,), (0,)), ((), ()))
contract_cols = (((1,), (1,)), ((), ()))


def silu_parts(pre_gate):
    sigmoid_gate = jax.nn.sigmoid(pre_gate)
    return (pre_gate * sigmoid_gate, sigmoid_gate * (1.0 + pre_gate * (1.0 - sigmoid_gate)))


def local_grads(pre_gate, pre_up, grad_act):
    active, slope_gate = silu_parts(pre_gate)
    hidden = (active * pre_up).astype(jnp.bfloat16)
    grad_gate = (grad_act * pre_up * slope_gate).astype(jnp.bfloat16)
    grad_up = (grad_act * active).astype(jnp.bfloat16)
    return (hidden, grad_gate, grad_up)


def shards(tokens, out_grad, expert_ids, gate_probs, w_gate, w_up, w_down):
    tok_rows, slab_width = tokens.shape
    owners = lax.axis_size("expert")
    experts = owners * w_gate.shape[0]
    pick_ids = expert_ids.T.reshape(-1)
    onehot = (pick_ids[:, None] == jnp.arange(experts, dtype=jnp.int32)[None, :]).astype(
        jnp.bfloat16
    )
    picks = pick_ids.shape[0]
    order = jnp.arange(picks, dtype=jnp.int32)
    earlier = (order[None, :] < order[:, None]).astype(jnp.bfloat16)
    before = jnp.dot(earlier, onehot, preferred_element_type=jnp.float32)
    rank_in = jnp.sum(before * onehot.astype(jnp.float32), axis=1).astype(jnp.int32)
    slot_of = pick_ids * MOST + rank_in
    placing = (jnp.arange(experts * MOST, dtype=jnp.int32)[:, None] == slot_of[None, :]).astype(
        jnp.bfloat16
    )
    row_pick = jnp.concatenate([tokens, tokens], axis=0)
    grad_pick = jnp.concatenate([out_grad, out_grad], axis=0)
    scaled = (gate_probs.T.reshape(-1)[:, None] * grad_pick.astype(jnp.float32)).astype(
        jnp.bfloat16
    )
    both = jnp.concatenate([row_pick, scaled], axis=1)
    send = (
        jnp.dot(placing, both, preferred_element_type=jnp.float32)
        .astype(jnp.bfloat16)
        .reshape(experts, MOST, 2 * slab_width)
    )
    arrived = lax.all_to_all(send, "expert", split_axis=0, concat_axis=0, tiled=True)
    arrived_tokens = arrived[:, :, :slab_width]
    arrived_grads = arrived[:, :, slab_width:]
    flat_tokens = arrived_tokens.reshape(-1, slab_width)
    flat_grads = arrived_grads.reshape(-1, slab_width)
    gate_mat = w_gate[0]
    up_mat = w_up[0]
    down_mat = w_down[0]
    part_gate = jnp.dot(flat_tokens, gate_mat, preferred_element_type=jnp.float32)
    part_up = jnp.dot(flat_tokens, up_mat, preferred_element_type=jnp.float32)
    part_act = lax.dot_general(
        flat_grads, down_mat, contract_cols, preferred_element_type=jnp.float32
    )
    pre_gate, pre_up, grad_act = (
        lax.psum(part_gate.astype(jnp.bfloat16), "dp").astype(jnp.float32),
        lax.psum(part_up.astype(jnp.bfloat16), "dp").astype(jnp.float32),
        lax.psum(part_act.astype(jnp.bfloat16), "dp").astype(jnp.float32),
    )
    hidden, grad_gate, grad_up = local_grads(pre_gate, pre_up, grad_act)
    grad_gate, grad_up = lax.optimization_barrier((grad_gate, grad_up))
    slot_grad = lax.dot_general(
        grad_gate, gate_mat, contract_cols, preferred_element_type=jnp.float32
    )
    slot_grad = slot_grad + lax.dot_general(
        grad_up, up_mat, contract_cols, preferred_element_type=jnp.float32
    )
    gate_grads = lax.dot_general(
        flat_tokens, grad_gate, contract_rows, preferred_element_type=jnp.float32
    )[None]
    up_grads = lax.dot_general(
        flat_tokens, grad_up, contract_rows, preferred_element_type=jnp.float32
    )[None]
    down_grads = lax.dot_general(
        hidden, flat_grads, contract_rows, preferred_element_type=jnp.float32
    )[None]
    returned = lax.all_to_all(
        slot_grad.reshape(experts, MOST, slab_width).astype(jnp.bfloat16),
        "expert",
        split_axis=0,
        concat_axis=0,
        tiled=True,
    )
    flat_back = returned.reshape(experts * MOST, slab_width)
    per_pick = lax.dot_general(
        placing, flat_back, contract_rows, preferred_element_type=jnp.float32
    )
    token_grad = (per_pick[:tok_rows] + per_pick[tok_rows:]).astype(jnp.bfloat16)
    return (token_grad, gate_grads, up_grads, down_grads)


def solution(mesh):
    in_specs = (
        P("expert", "dp"),
        P("expert", "dp"),
        P("expert", None),
        P("expert", None),
        P("expert", "dp", None),
        P("expert", "dp", None),
        P("expert", None, "dp"),
    )
    out_specs = (
        P("expert", "dp"),
        P("expert", "dp", None),
        P("expert", "dp", None),
        P("expert", None, "dp"),
    )
    return jax.shard_map(shards, mesh=mesh, in_specs=in_specs, out_specs=out_specs, check_vma=False)
```

profile of v0, /device:TPU:32, one launch (start us, length us, event | category | flops | bytes accessed | tf_op | source)
XLA Modules:
  0.0 285.1 jit_solution(2284455037294095577)
XLA Ops:
  7.2 0.0 copy-start
  7.2 0.0 all-reduce.3.cloned.1.call-start
  7.2 0.8 copy.11
  8.0 0.3 fusion.17
  8.3 0.7 copy.12
  9.0 1.2 multiply_convert_fusion
  10.2 2.3 fusion.13
  12.5 61.8 %all_to_all.10 = bf16[32,32,1024]{2,1,0:T(8,128)(2,1)S(1)} all-to-all(bf16[32,32,1024]{2,1,0:T(8,128)(2,1)S(1)} %bitcast.45), channel_id=1, replica_groups=mesh['dp'=8,'expert'=32] {'expert'}, dimensions={0} | all-to-all | bytes 4194304 | tf_op jit(solution)/shard_map/all_to_all | solution.py:52
  74.2 0.2 fusion.36
  74.4 0.0 copy-start.6
  74.5 0.0 copy-start.9
  74.5 2.6 convolution_convert_fusion
  77.1 2.6 convolution_convert_fusion.1
  79.6 2.6 convolution_convert_fusion.2
  82.2 0.0 all-reduce.3.cloned.1.call-update
  82.3 146.2 %all-reduce.3.cloned.1.call-done = (bf16[1024,1024]{1,0:T(8,128)(2,1)}, bf16[1024,1024]{1,0:T(8,128)(2,1)}, bf16[1024,1024]{1,0:T(8,128)(2,1)}) async-done(((bf16[1024,1024]{1,0:T(8,128)(2,1)}, bf16[1024,1024]{1,0:T(8,128)(2,1)}, bf16[1024,1024]{1,0:T(8,128)(2,1)}), (bf16[1024,1024]{1,0:T(8,128)(2,1)}, bf16[1024,1024]{1,0:T(8,128)(2,1)}, bf16[1024,1024]{1,0:T(8,128)(2,1)})) %all-reduce.3.cloned.1.call-update) | async-done | bytes 6291472 | tf_op jit(solution)/shard_map/psum | solution.py:67
  228.5 4.2 %fusion = (bf16[1024,1024]{1,0:T(8,128)(2,1)S(1)}, bf16[1024,1024]{1,0:T(8,128)(2,1)S(1)}) fusion(bf16[1024,1024]{1,0:T(8,128)(2,1)} %get-tuple-element.9, bf16[1024,1024]{1,0:T(8,128)(2,1)} %get-tuple-element.10, bf16[1024,1024]{1,0:T(8,128)(2,1)} %get-tuple-element.8), kind=kLoop, calls=%fused_computation.6 | loop fusion | flops 16777216 | bytes 10485760 | tf_op jit(solution)/shard_map/convert_element_type | solution.py:20
  232.8 0.0 copy-start.1
  232.8 0.0 copy-start.3
  232.8 1.3 fusion.23
  234.1 0.0 copy-done.1
  234.1 0.7 copy-done.3
  234.8 2.2 add_convert_fusion
  237.0 10.0 %all-to-all-start.1 = ((bf16[32,32,512]{2,1,0:T(8,128)(2,1)}), bf16[32,32,512]{2,1,0:T(8,128)(2,1)S(1)}, u32[]{:S(2)}, u32[]{:S(2)}) async-start(bf16[32,32,512]{2,1,0:T(8,128)(2,1)} %bitcast.47), calls=%async_computation.1 | async-start | bytes 2097152 | tf_op jit(solution)/shard_map/all_to_all | solution.py:87
  247.1 0.0 copy-start.2
  247.1 4.3 %convolution_bitcast_fusion.1 = f32[1,512,1024]{2,1,0:T(8,128)} fusion(bf16[1024,512]{1,0:T(8,128)(2,1)S(1)} %bitcast.43, bf16[1024,1024]{1,0:T(8,128)(2,1)} %copy-done.3), kind=kOutput, calls=%fused_computation.26 | convolution fusion | flops 1073741824 | bytes 5242880 | tf_op jit(solution)/shard_map/dot_general | solution.py:78
  251.4 2.6 convolution_bitcast_fusion
  254.0 0.6 copy-done.7
  254.6 2.8 fusion.14
  257.4 19.3 %all-to-all-done.1 = bf16[32,32,512]{2,1,0:T(8,128)(2,1)S(1)} async-done(((bf16[32,32,512]{2,1,0:T(8,128)(2,1)}), bf16[32,32,512]{2,1,0:T(8,128)(2,1)S(1)}, u32[]{:S(2)}, u32[]{:S(2)}) %all-to-all-start.1) | async-done | bytes 1048608 | tf_op jit(solution)/shard_map/all_to_all | solution.py:87
  276.7 0.8 fusion.11
  277.5 0.8 fusion.31
  (12 shorter events, 0.0 us)
Async XLA Ops:
  7.2 67.3 %copy-start = (bf16[1,512,1024]{2,1,0:T(8,128)(2,1)S(1)}, bf16[1,512,1024]{2,1,0:T(8,128)(2,1)}, u32[]{:S(2)}) copy-start(bf16[1,512,1024]{2,1,0:T(8,128)(2,1)} %param.11) | copy-start | bytes 3145732
  7.2 221.3 %all-reduce.3.cloned.1.call-start = ((), (), s32[]{:S(2)}) async-start(), calls=%async_computation.2 | async-start | bytes 12582912 | tf_op jit(solution)/shard_map/psum | solution.py:67
  74.4 5.2 %copy-start.6 = (bf16[32,32,512]{2,1,0:T(8,128)(2,1)}, bf16[32,32,512]{2,1,0:T(8,128)(2,1)S(1)}, u32[]{:S(2)}) copy-start(bf16[32,32,512]{2,1,0:T(8,128)(2,1)S(1)} %get-tuple-element.13) | copy-start | bytes 3145732
  74.5 2.6 copy-start.9
  77.1 2.6 copy-start.8
  232.8 1.3 copy-start.1
  232.8 2.0 copy-start.3
  237.0 39.7 %all-to-all-start.1 = ((bf16[32,32,512]{2,1,0:T(8,128)(2,1)}), bf16[32,32,512]{2,1,0:T(8,128)(2,1)S(1)}, u32[]{:S(2)}, u32[]{:S(2)}) async-start(bf16[32,32,512]{2,1,0:T(8,128)(2,1)} %bitcast.47), calls=%async_computation.1 | async-start | bytes 2097152 | tf_op jit(solution)/shard_map/all_to_all | solution.py:87
  247.1 4.3 %copy-start.2 = (bf16[1024,1024]{1,0:T(8,128)(2,1)S(1)}, bf16[1024,1024]{1,0:T(8,128)(2,1)}, u32[]{:S(2)}) copy-start(bf16[1024,1024]{1,0:T(8,128)(2,1)} %copy-done.1) | copy-start | bytes 6291460
  251.4 2.6 copy-start.4
  251.4 2.6 copy-start.5
  251.4 3.2 %copy-start.7 = (bf16[32,32,512]{2,1,0:T(8,128)(2,1)S(1)}, bf16[32,32,512]{2,1,0:T(8,128)(2,1)}, u32[]{:S(2)}) copy-start(bf16[32,32,512]{2,1,0:T(8,128)(2,1)} %copy-done.6) | copy-start | bytes 3145732
Sparse Core Ops, SparseCore 0:
  82.4 146.0 all-reduce.2
where the time goes:
time: 285 us
  waiting for transfers between devices  166 us (58%)
  blocking collectives  61.8 us (22%)
  matrix products  24.3 us (9%)
  between operations  14.2 us (5%)
  starting transfers between devices  10.1 us (4%)
  other arithmetic  6.21 us (2%)
  local copies, waits for them, and re-layouts  2.97 us (1%)
    psum x1, waiting for transfers between devices, shards(): lax.psum(part_up.astype(jnp.bfloat16), 'dp').astype(jnp.float32)  146 us
    all_to_all x1, blocking collectives, shards(): lax.all_to_all(send, 'expert', split_axis=0, concat_axis=0, tiled=True)  61.8 us
    all_to_all x1, waiting for transfers between devices, shards(): lax.all_to_all(slot_grad.reshape(experts, MOST, slab_width).astype(jnp.bf...  19.3 us
    all_to_all x1, starting transfers between devices, shards(): lax.all_to_all(slot_grad.reshape(experts, MOST, slab_width).astype(jnp.bf...  10 us
  transfers between devices with their start and end apart: 2, of which 2 were waited for; matrix products, arithmetic and copies ran while one was open for 3% of the time, Pallas kernels for 0%

commit v1 on v0

--- a/solution.py
+++ b/solution.py
@@ -64,7 +64,7 @@
     )
     pre_gate, pre_up, grad_act = (
         lax.psum(part_gate.astype(jnp.bfloat16), "dp").astype(jnp.float32),
-        lax.psum(part_up.astype(jnp.bfloat16), "dp").astype(jnp.float32),
+        jnp.sum(lax.all_gather(part_up.astype(jnp.bfloat16), "dp"), axis=0).astype(jnp.float32),
         lax.psum(part_act.astype(jnp.bfloat16), "dp").astype(jnp.float32),
     )
     hidden, grad_gate, grad_up = local_grads(pre_gate, pre_up, grad_act)

time: 285 us -> 417 us (1.46)
  waiting for transfers between devices: 166 us -> 285 us
  other arithmetic: 6.21 us -> 17 us
    all_gather x0 -> x1, waiting for transfers between devices: none -> 164 us  [shards(): lax.all_gather(part_up.astype(jnp.bfloat16), 'dp')]
    psum x1, waiting for transfers between devices: 146 us -> 102 us  [shards(): lax.psum(part_act.astype(jnp.bfloat16), 'dp').astype(jnp.float32)]
    reduce_sum x0 -> x1, other arithmetic: none -> 10.8 us  [shards(): jnp.sum(lax.all_gather(part_up.astype(jnp.bfloat16), 'dp'), axis=0)]
  transfers between devices with their start and end apart: 2 -> 3, of which waited for: 2 -> 3; matrix products, arithmetic and copies ran while one was open for 3% -> 6% of each run, Pallas kernels for 0% -> 0%
where the time goes in v1:
time: 417 us
  waiting for transfers between devices  285 us (68%)
  blocking collectives  61.8 us (15%)
  matrix products  24.4 us (6%)
  other arithmetic  17 us (4%)
  between operations  14.2 us (3%)
  starting transfers between devices  10.1 us (2%)
    all_gather x1, waiting for transfers between devices, shards(): lax.all_gather(part_up.astype(jnp.bfloat16), 'dp')  164 us
    psum x1, waiting for transfers between devices, shards(): lax.psum(part_act.astype(jnp.bfloat16), 'dp').astype(jnp.float32)  102 us
    all_to_all x1, blocking collectives, shards(): lax.all_to_all(send, 'expert', split_axis=0, concat_axis=0, tiled=True)  61.8 us
    all_to_all x1, waiting for transfers between devices, shards(): lax.all_to_all(slot_grad.reshape(experts, MOST, slab_width).astype(jnp.bf...  19.3 us
    reduce_sum x1, other arithmetic, shards(): jnp.sum(lax.all_gather(part_up.astype(jnp.bfloat16), 'dp'), axis=0)  10.8 us
    all_to_all x1, starting transfers between devices, shards(): lax.all_to_all(slot_grad.reshape(experts, MOST, slab_width).astype(jnp.bf...  10 us
  transfers between devices with their start and end apart: 3, of which 3 were waited for; matrix products, arithmetic and copies ran while one was open for 6% of the time, Pallas kernels for 0%

profile of v1, /device:TPU:32, one launch (start us, length us, event | category | flops | bytes accessed | tf_op | source)
XLA Modules:
  0.0 416.6 jit_solution(15794422687783754138)
XLA Ops:
  7.2 0.0 copy-start
  7.2 0.0 all-gather.3.cloned.1.call-start
  7.2 0.8 copy.11
  8.0 0.3 fusion.17
  8.3 0.7 copy.12
  9.0 1.2 multiply_convert_fusion
  10.2 2.3 fusion.13
  12.5 61.8 %all_to_all.10 = bf16[32,32,1024]{2,1,0:T(8,128)(2,1)S(1)} all-to-all(bf16[32,32,1024]{2,1,0:T(8,128)(2,1)S(1)} %bitcast.47), channel_id=1, replica_groups=mesh['dp'=8,'expert'=32] {'expert'}, dimensions={0} | all-to-all | bytes 4194304 | tf_op jit(solution)/shard_map/all_to_all | solution.py:52
  74.2 0.3 fusion.36
  74.6 0.9 copy-done.9
  75.5 2.6 convolution_convert_fusion.1
  78.0 0.0 all-gather.3.cloned.1.call-update
  78.1 0.0 all-reduce.3.cloned.1.call-start
  78.1 2.6 convolution_convert_fusion
  80.7 2.6 convolution_convert_fusion.2
  83.3 0.0 all-reduce.3.cloned.1.call-update
  83.3 164.1 %all-gather.3.cloned.1.call-done = bf16[8192,1024]{1,0:T(8,128)(2,1)} async-done(((bf16[1024,1024]{1,0:T(8,128)(2,1)}), bf16[8192,1024]{1,0:T(8,128)(2,1)}) %all-gather.3.cloned.1.call-update) | async-done | bytes 16777232 | tf_op jit(solution)/shard_map/all_gather | solution.py:67
  247.4 10.8 %reduce_sum.22 = bf16[1024,1024]{1,0:T(8,128)(2,1)} reduce(bf16[8,1024,1024]{2,1,0:T(8,128)(2,1)} %bitcast.42, bf16[]{:T(256)} %constant.6.clone.1), dimensions={0}, to_apply=%region_2.0 | reduce | flops 7340032 | bytes 18874370 | tf_op jit(solution)/shard_map/reduce_sum | solution.py:67
  258.2 101.7 %all-reduce.3.cloned.1.call-done = (bf16[1024,1024]{1,0:T(8,128)(2,1)}, bf16[1024,1024]{1,0:T(8,128)(2,1)}) async-done(((bf16[1024,1024]{1,0:T(8,128)(2,1)}, bf16[1024,1024]{1,0:T(8,128)(2,1)}), (bf16[1024,1024]{1,0:T(8,128)(2,1)}, bf16[1024,1024]{1,0:T(8,128)(2,1)})) %all-reduce.3.cloned.1.call-update) | async-done | bytes 4194320 | tf_op jit(solution)/shard_map/psum | solution.py:68
  360.0 4.2 %fusion = (bf16[1024,1024]{1,0:T(8,128)(2,1)S(1)}, bf16[1024,1024]{1,0:T(8,128)(2,1)S(1)}) fusion(bf16[1024,1024]{1,0:T(8,128)(2,1)} %get-tuple-element.8, bf16[1024,1024]{1,0:T(8,128)(2,1)} %get-tuple-element.9, bf16[1024,1024]{1,0:T(8,128)(2,1)} %reduce_sum.22), kind=kLoop, calls=%fused_computation.6 | loop fusion | flops 16777216 | bytes 10485760 | tf_op jit(solution)/shard_map/convert_element_type | solution.py:20
  364.2 1.3 fusion.23
  365.5 0.7 copy-done.3
  366.2 0.0 copy-done.10
  366.3 2.3 add_convert_fusion
  368.5 10.0 %all-to-all-start.1 = ((bf16[32,32,512]{2,1,0:T(8,128)(2,1)}), bf16[32,32,512]{2,1,0:T(8,128)(2,1)S(1)}, u32[]{:S(2)}, u32[]{:S(2)}) async-start(bf16[32,32,512]{2,1,0:T(8,128)(2,1)} %bitcast.49), calls=%async_computation.1 | async-start | bytes 2097152 | tf_op jit(solution)/shard_map/all_to_all | solution.py:87
  378.6 4.3 %convolution_bitcast_fusion.1 = f32[1,512,1024]{2,1,0:T(8,128)} fusion(bf16[1024,512]{1,0:T(8,128)(2,1)S(1)} %bitcast.45, bf16[1024,1024]{1,0:T(8,128)(2,1)} %copy-done.3), kind=kOutput, calls=%fused_computation.26 | convolution fusion | flops 1073741824 | bytes 5242880 | tf_op jit(solution)/shard_map/dot_general | solution.py:78
  382.9 2.6 convolution_bitcast_fusion
  385.5 0.6 copy-done.7
  386.1 2.8 fusion.14
  388.9 19.3 %all-to-all-done.1 = bf16[32,32,512]{2,1,0:T(8,128)(2,1)S(1)} async-done(((bf16[32,32,512]{2,1,0:T(8,128)(2,1)}), bf16[32,32,512]{2,1,0:T(8,128)(2,1)S(1)}, u32[]{:S(2)}, u32[]{:S(2)}) %all-to-all-start.1) | async-done | bytes 1048608 | tf_op jit(solution)/shard_map/all_to_all | solution.py:87
  408.2 0.8 fusion.11
  409.0 0.8 fusion.31
  (18 shorter events, 0.1 us)
Async XLA Ops:
  7.2 71.0 %copy-start = (bf16[1,512,1024]{2,1,0:T(8,128)(2,1)S(1)}, bf16[1,512,1024]{2,1,0:T(8,128)(2,1)}, u32[]{:S(2)}) copy-start(bf16[1,512,1024]{2,1,0:T(8,128)(2,1)} %param.11) | copy-start | bytes 3145732
  7.2 240.2 %all-gather.3.cloned.1.call-start = ((), (), s32[]{:S(2)}) async-start(), calls=%async_computation.2 | async-start | bytes 18874368 | tf_op jit(solution)/shard_map/all_gather | solution.py:67
  74.2 1.2 copy-start.9
  74.5 6.2 %copy-start.6 = (bf16[32,32,512]{2,1,0:T(8,128)(2,1)}, bf16[32,32,512]{2,1,0:T(8,128)(2,1)S(1)}, u32[]{:S(2)}) copy-start(bf16[32,32,512]{2,1,0:T(8,128)(2,1)S(1)} %get-tuple-element.12) | copy-start | bytes 3145732
  78.1 281.9 %all-reduce.3.cloned.1.call-start = ((), (), s32[]{:S(2)}) async-start(), calls=%async_computation.3 | async-start | bytes 8388608 | tf_op jit(solution)/shard_map/psum | solution.py:68
  78.1 2.6 copy-start.8
  364.2 1.3 copy-start.1
  364.2 2.0 copy-start.3
  364.2 2.0 copy-start.10
  368.5 39.7 %all-to-all-start.1 = ((bf16[32,32,512]{2,1,0:T(8,128)(2,1)}), bf16[32,32,512]{2,1,0:T(8,128)(2,1)S(1)}, u32[]{:S(2)}, u32[]{:S(2)}) async-start(bf16[32,32,512]{2,1,0:T(8,128)(2,1)} %bitcast.49), calls=%async_computation.1 | async-start | bytes 2097152 | tf_op jit(solution)/shard_map/all_to_all | solution.py:87
  378.6 4.3 %copy-start.2 = (bf16[1024,1024]{1,0:T(8,128)(2,1)S(1)}, bf16[1024,1024]{1,0:T(8,128)(2,1)}, u32[]{:S(2)}) copy-start(bf16[1024,1024]{1,0:T(8,128)(2,1)} %copy-done.1) | copy-start | bytes 6291460
  382.9 2.6 copy-start.4
  382.9 2.6 copy-start.5
  382.9 3.2 copy-start.7
Sparse Core Ops, SparseCore 0:
  78.2 169.1 all-gather.2
  250.7 109.2 all-reduce.2
